TPU v7x, 256 devices: a whole 4x4x8 slice. The times are simulated.
256 devices in a mesh: space: 16 (over x_hi, z), chan: 8 (over y, core), dp: 2 (over x_lo).
Axes of the slice: x: 4 (x_hi: 2, x_lo: 2; x = x_hi * 2 + x_lo), y: 4, z: 8, core: 2. Of those that a mesh axis runs over, the one named last changes fastest.
Arguments:
- inputs: bfloat16 [2, 32, 8, 128, 512], P('dp', 'space', None, 'chan'), may hold values from -6 to 6
- cotangent: bfloat16 [2, 32, 8, 128, 512], P('dp', 'space', None, 'chan'), may hold values from -6 to 6
- weight: bfloat16 [27, 128, 128], P(None, 'chan'), may hold values from -0.109375 to 0.109375
Outputs:
- input_grad: bfloat16 [2, 32, 8, 128, 512], P('dp', 'space', None, 'chan')
- weight_grad: float32 [27, 128, 128], P(None, 'chan')
All inputs are finite; a program needn't handle non-finite values.
Results may differ from a plain program's by a relative error of at most 0.001.
Values may be sent and summed in bfloat16 or wider, within the bound.
No kernel may reach another device: no remote copies, remote signals or barrier semaphores. Data moves between devices by JAX's collectives and lax.ppermute only.
A program may use at most 64 MiB of HBM per device.

v0:
```python
import math
import jax
import jax.numpy as jnp
from jax import lax
from jax.sharding import PartitionSpec as P


def from_behind(value, axis, steps):
    count = lax.axis_size(axis)
    initial, last = (max(0, -steps), min(count, count - steps))
    return lax.ppermute(value, axis, [(source, source + steps) for source in range(initial, last)])


def exchange_sum(value, axis, distance):
    count = lax.axis_size(axis)
    return value + lax.ppermute(value, axis, [(i, i ^ distance) for i in range(count)])


def butterfly_sum(value):
    value = exchange_sum(value, "dp", 1)
    for distance in (1, 8, 2, 4):
        value = exchange_sum(value, "space", distance)
    return value


def shift_cells(block, step_z, step_y):
    zero = jnp.zeros((), block.dtype)
    config = ((0, 0, 0), (0, 0, 0), (step_z, -step_z, 0), (0, 0, 0), (step_y, -step_y, 0))
    return lax.pad(block, zero, config)


def local(inputs, cotangent, weight):
    samples, planes, depth, channels, width = inputs.shape
    outputs = weight.shape[2]
    gathered = lax.all_gather(cotangent, "chan", axis=3, tiled=True)
    lower_plane = from_behind(gathered[:, -1:], "space", 1)
    upper_plane = from_behind(gathered[:, :1], "space", -1)
    stacked = jnp.concatenate(
        [shift_cells(inputs, -step_z, -step_y) for step_z in (-1, 0, 1) for step_y in (-1, 0, 1)],
        axis=3,
    )
    accum = jnp.zeros(inputs.shape, jnp.float32)
    groups = []
    for step_x in (-1, 0, 1):
        if step_x == 1:
            slab = jnp.concatenate([lower_plane, gathered[:, : planes - 1]], axis=1)
        elif step_x == -1:
            slab = jnp.concatenate([gathered[:, 1:], upper_plane], axis=1)
        else:
            slab = gathered
        first = 9 * (step_x + 1)
        groups.append(
            jnp.einsum("bxzky,bxzcy->kc", stacked, slab, preferred_element_type=jnp.float32)
        )
        for step_y in (-1, 0, 1):
            kernel = weight[first + step_y + 1 : first + 9 : 3].reshape(3 * channels, outputs)
            product = jnp.einsum(
                "bxzcy,kc->bxzky", slab, kernel, preferred_element_type=jnp.float32
            )
            for place, step_z in enumerate((-1, 0, 1)):
                part = product[:, :, :, place * channels : (place + 1) * channels]
                accum = accum + shift_cells(part, step_z, step_y)
    input_grad = accum.astype(jnp.bfloat16)
    local_grad = jnp.concatenate(groups, axis=0).reshape(27, channels, outputs)
    count = samples * lax.axis_size("dp") * planes * lax.axis_size("space") * depth * width
    scale = 1.0 / math.sqrt(count)
    weight_grad = butterfly_sum(local_grad) * scale
    return (input_grad, weight_grad)


def solution(mesh):
    placed = (
        P("dp", "space", None, "chan", None),
        P("dp", "space", None, "chan", None),
        P(None, "chan", None),
    )
    return jax.shard_map(
        local,
        mesh=mesh,
        in_specs=placed,
        out_specs=(P("dp", "space", None, "chan", None), P(None, "chan", None)),
        check_vma=False,
    )
```

profile of v0, /device:TPU:4, one launch (start us, length us, event | category | flops | bytes accessed | tf_op | source)
XLA Modules:
  0.0 135.7 jit_solution(2542420532690271903)
XLA Ops:
  7.2 0.7 all-gather.2.cloned.1.call-update
  7.9 1.1 fusion.64
  9.0 1.0 fusion.60
  10.0 1.1 fusion.65
  11.1 1.1 fusion.62
  12.7 28.0 %all-gather.2.cloned.1.call-done = bf16[1,2,8,128,512]{4,3,2,1,0:T(8,128)(2,1)} async-done(((bf16[1,2,8,16,512]{4,3,2,1,0:T(8,128)(2,1)}), bf16[1,2,8,128,512]{4,3,2,1,0:T(8,128)(2,1)}) %all-gather.2.cloned.1.call-update) | async-done | bytes 2097168 | tf_op jit(solution)/shard_map/all_gather | solution.py:35
  40.7 1.9 %fusion.68 = (bf16[1,1,8,128,512]{4,3,2,1,0:T(8,128)(2,1)S(1)}, bf16[1,1,8,128,512]{4,3,2,1,0:T(8,128)(2,1)S(1)}) fusion(bf16[1,2,8,128,512]{4,3,2,1,0:T(8,128)(2,1)} %all-gather.2.cloned.1.call-done), kind=kLoop, calls=%fused_computation.97 | loop fusion | bytes 4194304 | tf_op jit(solution)/shard_map/slice | solution.py:48
  42.6 5.2 %collective-permute-start = (bf16[1,1,8,128,512]{4,3,2,1,0:T(8,128)(2,1)S(1)}, bf16[1,1,8,128,512]{4,3,2,1,0:T(8,128)(2,1)S(1)}, u32[]{:S(2)}, u32[]{:S(2)}) collective-permute-start(bf16[1,1,8,128,512]{4,3,2,1,0:T(8,128)(2,1)S(1)} %get-tuple-element.3), channel_id=1, source_target_pairs={{16,0},{32,16},{48,32},{64,48},{80,64},{96,80},{112,96},{128,112},... | collective-permute-start | bytes 3145736 | tf_op jit(solution)/shard_map/ppermute | solution.py:11
  47.8 1.9 %collective-permute-start.1 = (bf16[1,1,8,128,512]{4,3,2,1,0:T(8,128)(2,1)S(1)}, bf16[1,1,8,128,512]{4,3,2,1,0:T(8,128)(2,1)S(1)}, u32[]{:S(2)}, u32[]{:S(2)}) collective-permute-start(bf16[1,1,8,128,512]{4,3,2,1,0:T(8,128)(2,1)S(1)} %get-tuple-element.2), channel_id=1, source_target_pairs={{0,16},{16,32},{32,48},{48,64},{64,80},{80,96},{96,112},{112,128},... | collective-permute-start | bytes 3145736 | tf_op jit(solution)/shard_map/ppermute | solution.py:11
  50.7 0.4 fusion.13
  51.1 0.4 fusion.72
  51.5 0.8 fusion.25
  52.3 18.3 %collective-permute-done = bf16[1,1,8,128,512]{4,3,2,1,0:T(8,128)(2,1)S(1)} collective-permute-done((bf16[1,1,8,128,512]{4,3,2,1,0:T(8,128)(2,1)S(1)}, bf16[1,1,8,128,512]{4,3,2,1,0:T(8,128)(2,1)S(1)}, u32[]{:S(2)}, u32[]{:S(2)}) %collective-permute-start) | collective-permute-done | bytes 1048608 | tf_op jit(solution)/shard_map/ppermute | solution.py:11
  70.6 0.8 fusion.22
  71.3 7.1 %collective-permute-done.1 = bf16[1,1,8,128,512]{4,3,2,1,0:T(8,128)(2,1)S(1)} collective-permute-done((bf16[1,1,8,128,512]{4,3,2,1,0:T(8,128)(2,1)S(1)}, bf16[1,1,8,128,512]{4,3,2,1,0:T(8,128)(2,1)S(1)}, u32[]{:S(2)}, u32[]{:S(2)}) %collective-permute-start.1) | collective-permute-done | bytes 1048608 | tf_op jit(solution)/shard_map/ppermute | solution.py:11
  78.4 0.8 fusion.30
  79.2 2.2 %collective-permute-start.2 = (f32[27,16,128]{2,1,0:T(8,128)S(1)}, f32[27,16,128]{2,1,0:T(8,128)S(1)}, u32[]{:S(2)}, u32[]{:S(2)}) collective-permute-start(f32[27,16,128]{2,1,0:T(8,128)S(1)} %bitcast.157), channel_id=1, source_target_pairs={{0,1},{1,0},{2,3},{3,2},{4,5},{5,4},{6,7},{7,6},{8,9},{9,8},{10,11... | collective-permute-start | bytes 663560 | tf_op jit(solution)/shard_map/ppermute | solution.py:16
  81.4 0.4 convolution_bitcast_fusion.4
  81.8 0.4 convolution_bitcast_fusion.5
  82.2 0.4 fusion.69
  82.6 0.4 convolution_bitcast_fusion.1
  83.1 0.4 convolution_bitcast_fusion.2
  83.5 2.5 %collective-permute-done.2 = f32[27,16,128]{2,1,0:T(8,128)S(1)} collective-permute-done((f32[27,16,128]{2,1,0:T(8,128)S(1)}, f32[27,16,128]{2,1,0:T(8,128)S(1)}, u32[]{:S(2)}, u32[]{:S(2)}) %collective-permute-start.2) | collective-permute-done | bytes 221216 | tf_op jit(solution)/shard_map/ppermute | solution.py:16
  86.1 0.4 fusion.75
  86.5 0.4 convolution_bitcast_fusion.3
  87.0 5.1 %collective-permute-done.3 = f32[27,16,128]{2,1,0:T(8,128)S(1)} collective-permute-done((f32[27,16,128]{2,1,0:T(8,128)S(1)}, f32[27,16,128]{2,1,0:T(8,128)S(1)}, u32[]{:S(2)}, u32[]{:S(2)}) %collective-permute-start.3) | collective-permute-done | bytes 221216 | tf_op jit(solution)/shard_map/ppermute | solution.py:16
  92.3 0.4 convolution_bitcast_fusion
  92.7 6.9 %collective-permute-done.4 = f32[27,16,128]{2,1,0:T(8,128)S(1)} collective-permute-done((f32[27,16,128]{2,1,0:T(8,128)S(1)}, f32[27,16,128]{2,1,0:T(8,128)S(1)}, u32[]{:S(2)}, u32[]{:S(2)}) %collective-permute-start.4) | collective-permute-done | bytes 221216 | tf_op jit(solution)/shard_map/ppermute | solution.py:16
  99.8 18.3 %collective-permute-done.5 = f32[27,16,128]{2,1,0:T(8,128)S(1)} collective-permute-done((f32[27,16,128]{2,1,0:T(8,128)S(1)}, f32[27,16,128]{2,1,0:T(8,128)S(1)}, u32[]{:S(2)}, u32[]{:S(2)}) %collective-permute-start.5) | collective-permute-done | bytes 221216 | tf_op jit(solution)/shard_map/ppermute | solution.py:16
  118.3 3.4 %fusion.59 = bf16[1,2,8,16,512]{4,3,2,1,0:T(8,128)(2,1)} fusion(f32[1,2,8,16,512]{4,3,2,1,0:T(8,128)S(1)} %get-tuple-element.26, f32[1,2,8,16,512]{4,3,2,1,0:T(8,128)S(1)} %get-tuple-element.27, f32[1,2,8,16,512]{4,3,2,1,0:T(8,128)S(1)} %get-tuple-element.25, f32[1,2,8,16,512]{4,3,2,1,0:T(8,128)S(1)} %get-tuple-element.41, ...), kind=kLoop, calls=%fused_computation.77 | loop fusion | flops 3538944 | bytes 14417920 | tf_op jit(solution)/shard_map/convert_element_type | solution.py:63
  121.7 6.4 %collective-permute-done.6 = f32[27,16,128]{2,1,0:T(8,128)S(1)} collective-permute-done((f32[27,16,128]{2,1,0:T(8,128)S(1)}, f32[27,16,128]{2,1,0:T(8,128)S(1)}, u32[]{:S(2)}, u32[]{:S(2)}) %collective-permute-start.6) | collective-permute-done | bytes 221216 | tf_op jit(solution)/shard_map/ppermute | solution.py:16
  128.1 0.7 add_multiply_fusion
  (27 shorter events, 2.2 us)
Async XLA Ops:
  7.2 5.0 %copy-start.1 = (bf16[1,2,8,16,512]{4,3,2,1,0:T(8,128)(2,1)S(1)}, bf16[1,2,8,16,512]{4,3,2,1,0:T(8,128)(2,1)}, u32[]{:S(2)}) copy-start(bf16[1,2,8,16,512]{4,3,2,1,0:T(8,128)(2,1)} %param.3) | copy-start | bytes 786436
  7.2 33.5 %all-gather.2.cloned.1.call-start = ((), (), s32[]{:S(2)}) async-start(), calls=%async_computation | async-start | bytes 2359296 | tf_op jit(solution)/shard_map/all_gather | solution.py:35
  9.0 3.7 %copy-start.2 = (bf16[27,16,128]{2,1,0:T(8,128)(2,1)S(1)}, bf16[27,16,128]{2,1,0:T(8,128)(2,1)}, u32[]{:S(2)}) copy-start(bf16[27,16,128]{2,1,0:T(8,128)(2,1)} %param.5) | copy-start | bytes 331780
  40.7 9.0 %copy-start = (bf16[1,2,8,128,512]{4,3,2,1,0:T(8,128)(2,1)S(1)}, bf16[1,2,8,128,512]{4,3,2,1,0:T(8,128)(2,1)}, u32[]{:S(2)}) copy-start(bf16[1,2,8,128,512]{4,3,2,1,0:T(8,128)(2,1)} %all-gather.2.cloned.1.call-done) | copy-start | bytes 6291460
  42.6 28.0 %collective-permute-start = (bf16[1,1,8,128,512]{4,3,2,1,0:T(8,128)(2,1)S(1)}, bf16[1,1,8,128,512]{4,3,2,1,0:T(8,128)(2,1)S(1)}, u32[]{:S(2)}, u32[]{:S(2)}) collective-permute-start(bf16[1,1,8,128,512]{4,3,2,1,0:T(8,128)(2,1)S(1)} %get-tuple-element.3), channel_id=1, source_target_pairs={{16,0},{32,16},{48,32},{64,48},{80,64},{96,80},{112,96},{128,112},... | collective-permute-start | bytes 3145736 | tf_op jit(solution)/shard_map/ppermute | solution.py:11
  47.8 30.6 %collective-permute-start.1 = (bf16[1,1,8,128,512]{4,3,2,1,0:T(8,128)(2,1)S(1)}, bf16[1,1,8,128,512]{4,3,2,1,0:T(8,128)(2,1)S(1)}, u32[]{:S(2)}, u32[]{:S(2)}) collective-permute-start(bf16[1,1,8,128,512]{4,3,2,1,0:T(8,128)(2,1)S(1)} %get-tuple-element.2), channel_id=1, source_target_pairs={{0,16},{16,32},{32,48},{48,64},{64,80},{80,96},{96,112},{112,128},... | collective-permute-start | bytes 3145736 | tf_op jit(solution)/shard_map/ppermute | solution.py:11
  79.2 6.8 %collective-permute-start.2 = (f32[27,16,128]{2,1,0:T(8,128)S(1)}, f32[27,16,128]{2,1,0:T(8,128)S(1)}, u32[]{:S(2)}, u32[]{:S(2)}) collective-permute-start(f32[27,16,128]{2,1,0:T(8,128)S(1)} %bitcast.157), channel_id=1, source_target_pairs={{0,1},{1,0},{2,3},{3,2},{4,5},{5,4},{6,7},{7,6},{8,9},{9,8},{10,11... | collective-permute-start | bytes 663560 | tf_op jit(solution)/shard_map/ppermute | solution.py:16
  86.0 6.0 %collective-permute-start.3 = (f32[27,16,128]{2,1,0:T(8,128)S(1)}, f32[27,16,128]{2,1,0:T(8,128)S(1)}, u32[]{:S(2)}, u32[]{:S(2)}) collective-permute-start(f32[27,16,128]{2,1,0:T(8,128)S(1)} %add.183), channel_id=1, source_target_pairs={{0,16},{16,0},{32,48},{48,32},{64,80},{80,64},{96,112},{112,96},{1... | collective-permute-start | bytes 663560 | tf_op jit(solution)/shard_map/ppermute | solution.py:16
  92.1 7.5 %collective-permute-start.4 = (f32[27,16,128]{2,1,0:T(8,128)S(1)}, f32[27,16,128]{2,1,0:T(8,128)S(1)}, u32[]{:S(2)}, u32[]{:S(2)}) collective-permute-start(f32[27,16,128]{2,1,0:T(8,128)S(1)} %add.184), channel_id=1, source_target_pairs={{0,128},{16,144},{32,160},{48,176},{64,192},{80,208},{96,224},{112... | collective-permute-start | bytes 663560 | tf_op jit(solution)/shard_map/ppermute | solution.py:16
  99.6 18.6 %collective-permute-start.5 = (f32[27,16,128]{2,1,0:T(8,128)S(1)}, f32[27,16,128]{2,1,0:T(8,128)S(1)}, u32[]{:S(2)}, u32[]{:S(2)}) collective-permute-start(f32[27,16,128]{2,1,0:T(8,128)S(1)} %add.185), channel_id=1, source_target_pairs={{0,32},{16,48},{32,0},{48,16},{64,96},{80,112},{96,64},{112,80},{1... | collective-permute-start | bytes 663560 | tf_op jit(solution)/shard_map/ppermute | solution.py:16
  118.2 9.9 %collective-permute-start.6 = (f32[27,16,128]{2,1,0:T(8,128)S(1)}, f32[27,16,128]{2,1,0:T(8,128)S(1)}, u32[]{:S(2)}, u32[]{:S(2)}) collective-permute-start(f32[27,16,128]{2,1,0:T(8,128)S(1)} %add.186), channel_id=1, source_target_pairs={{0,64},{16,80},{32,96},{48,112},{64,0},{80,16},{96,32},{112,48},{1... | collective-permute-start | bytes 663560 | tf_op jit(solution)/shard_map/ppermute | solution.py:16
Sparse Core Ops, SparseCore 0:
  9.8 30.7 all-gather.1
where the time goes:
time: 136 us
  waiting for transfers between devices  93.1 us (68%)
  between operations  14.3 us (11%)
  starting transfers between devices  9.7 us (7%)
  local copies, waits for them, and re-layouts  8.23 us (6%)
  matrix products  6.09 us (4%)
  other arithmetic  4.23 us (3%)
    ppermute x5, waiting for transfers between devices, exchange_sum(): lax.ppermute(value, axis, [(i, i ^ distance) for i in range(count)])  39.2 us
    all_gather x1, waiting for transfers between devices, local(): gathered = lax.all_gather(cotangent, 'chan', axis=3, tiled=True)  28 us
    ppermute x2, waiting for transfers between devices, from_behind(): lax.ppermute(value, axis, [(source, source + steps) for source in range(i...  25.3 us
    ppermute x2, starting transfers between devices, from_behind(): lax.ppermute(value, axis, [(source, source + steps) for source in range(i...  7.13 us
    unnamed x14, local copies, waits for them, and re-layouts  4.55 us
    dot_general x9, matrix products, local(): jnp.einsum('bxzcy,kc->bxzky', slab, kernel, preferred_element_type=jnp.fl...  3.78 us
    convert_element_type x1, other arithmetic, local(): input_grad = accum.astype(jnp.bfloat16)  3.38 us
  transfers between devices with their start and end apart: 8, of which 8 were waited for; matrix products, arithmetic and copies ran while one was open for 11% of the time, Pallas kernels for 0%

commit v1 on v0

--- a/solution.py
+++ b/solution.py
@@ -32,7 +32,9 @@
 def local(inputs, cotangent, weight):
     samples, planes, depth, channels, width = inputs.shape
     outputs = weight.shape[2]
-    gathered = lax.all_gather(cotangent, "chan", axis=3, tiled=True)
+    gathered = jnp.concatenate(
+        lax.all_to_all(jnp.stack([cotangent] * lax.axis_size("chan")), "chan", 0, 0), axis=3
+    )
     lower_plane = from_behind(gathered[:, -1:], "space", 1)
     upper_plane = from_behind(gathered[:, :1], "space", -1)
     stacked = jnp.concatenate(

time: 136 us -> 116 us (0.85)
  the two profiles are of different devices: /device:TPU:4 before, /device:TPU:224 now
where the time goes in v1:
time: 116 us
  waiting for transfers between devices  83.5 us (72%)
  starting transfers between devices  12.9 us (11%)
  local copies, waits for them, and re-layouts  8.22 us (7%)
  matrix products  6.09 us (5%)
  other arithmetic  4.21 us (4%)
    ppermute x5, waiting for transfers between devices, exchange_sum(): lax.ppermute(value, axis, [(i, i ^ distance) for i in range(count)])  37.1 us
    all_to_all x1, waiting for transfers between devices, local(): lax.all_to_all(jnp.stack([cotangent] * lax.axis_size('chan')), 'chan', 0, 0)  24.8 us
    ppermute x2, waiting for transfers between devices, from_behind(): lax.ppermute(value, axis, [(source, source + steps) for source in range(i...  21.6 us
    ppermute x2, starting transfers between devices, from_behind(): lax.ppermute(value, axis, [(source, source + steps) for source in range(i...  5.84 us
    all_to_all x1, starting transfers between devices, local(): lax.all_to_all(jnp.stack([cotangent] * lax.axis_size('chan')), 'chan', 0, 0)  4.6 us
    dot_general x9, matrix products, local(): jnp.einsum('bxzcy,kc->bxzky', slab, kernel, preferred_element_type=jnp.fl...  3.8 us
    unnamed x16, local copies, waits for them, and re-layouts  3.37 us
    convert_element_type x1, other arithmetic, local(): input_grad = accum.astype(jnp.bfloat16)  3.37 us
  transfers between devices with their start and end apart: 8, of which 8 were waited for; matrix products, arithmetic and copies ran while one was open for 10% of the time, Pallas kernels for 0%

profile of v1, /device:TPU:224, one launch (start us, length us, event | category | flops | bytes accessed | tf_op | source)
XLA Modules:
  0.0 115.8 jit_solution(2701968775409882286)
XLA Ops:
  0.6 2.5 %stack.2 = bf16[8,1,2,8,16,512]{5,4,3,2,1,0:T(8,128)(2,1)} broadcast(bf16[2,8,16,512]{3,2,1,0:T(8,128)(2,1)} %bitcast.156), dimensions={2,3,4,5} | broadcast | bytes 2359296 | tf_op jit(solution)/shard_map/stack | solution.py:36
  3.2 4.6 %all-to-all-start = ((bf16[8,1,2,8,16,512]{5,4,3,2,1,0:T(8,128)(2,1)}), bf16[8,1,2,8,16,512]{5,4,3,2,1,0:T(8,128)(2,1)S(1)}, u32[]{:S(2)}, u32[]{:S(2)}) async-start(bf16[8,1,2,8,16,512]{5,4,3,2,1,0:T(8,128)(2,1)} %stack.2), calls=%async_computation | async-start | bytes 4194304 | tf_op jit(solution)/shard_map/all_to_all | solution.py:36
  8.7 1.4 %copy-done.1 = bf16[1,2,8,144,512]{4,3,2,1,0:T(8,128)(2,1)} copy-done((bf16[1,2,8,144,512]{4,3,2,1,0:T(8,128)(2,1)}, bf16[1,2,8,144,512]{4,3,2,1,0:T(8,128)(2,1)S(1)}, u32[]{:S(2)}) %copy-start.1) | copy-done | bytes 2359320
  10.1 24.8 %all-to-all-done = bf16[8,1,2,8,16,512]{5,4,3,2,1,0:T(8,128)(2,1)S(1)} async-done(((bf16[8,1,2,8,16,512]{5,4,3,2,1,0:T(8,128)(2,1)}), bf16[8,1,2,8,16,512]{5,4,3,2,1,0:T(8,128)(2,1)S(1)}, u32[]{:S(2)}, u32[]{:S(2)}) %all-to-all-start) | async-done | bytes 2097184 | tf_op jit(solution)/shard_map/all_to_all | solution.py:36
  35.3 1.9 %collective-permute-start.1 = (bf16[1,1,8,128,512]{4,3,2,1,0:T(8,128)(2,1)S(1)}, bf16[1,1,8,128,512]{4,3,2,1,0:T(8,128)(2,1)S(1)}, u32[]{:S(2)}, u32[]{:S(2)}) collective-permute-start(bf16[1,1,8,128,512]{4,3,2,1,0:T(8,128)(2,1)S(1)} %get-tuple-element.2), channel_id=1, source_target_pairs={{0,16},{16,32},{32,48},{48,64},{64,80},{80,96},{96,112},{112,128},... | collective-permute-start | bytes 3145736 | tf_op jit(solution)/shard_map/ppermute | solution.py:11
  37.3 3.9 %collective-permute-start = (bf16[1,1,8,128,512]{4,3,2,1,0:T(8,128)(2,1)S(1)}, bf16[1,1,8,128,512]{4,3,2,1,0:T(8,128)(2,1)S(1)}, u32[]{:S(2)}, u32[]{:S(2)}) collective-permute-start(bf16[1,1,8,128,512]{4,3,2,1,0:T(8,128)(2,1)S(1)} %get-tuple-element.3), channel_id=1, source_target_pairs={{16,0},{32,16},{48,32},{64,48},{80,64},{96,80},{112,96},{128,112},... | collective-permute-start | bytes 3145736 | tf_op jit(solution)/shard_map/ppermute | solution.py:11
  41.2 0.4 convolution_bitcast_fusion.6
  41.7 0.4 convolution_bitcast_fusion.7
  42.2 0.4 convolution_bitcast_fusion.8
  42.6 0.4 fusion.54
  43.0 1.2 %copy-done.2 = bf16[1,2,8,144,512]{4,3,2,1,0:T(8,128)(2,1)S(1)} copy-done((bf16[1,2,8,144,512]{4,3,2,1,0:T(8,128)(2,1)S(1)}, bf16[1,2,8,144,512]{4,3,2,1,0:T(8,128)(2,1)}, u32[]{:S(2)}) %copy-start.2) | copy-done | bytes 2359320
  44.3 0.8 fusion.9
  45.0 16.8 %collective-permute-done.1 = bf16[1,1,8,128,512]{4,3,2,1,0:T(8,128)(2,1)S(1)} collective-permute-done((bf16[1,1,8,128,512]{4,3,2,1,0:T(8,128)(2,1)S(1)}, bf16[1,1,8,128,512]{4,3,2,1,0:T(8,128)(2,1)S(1)}, u32[]{:S(2)}, u32[]{:S(2)}) %collective-permute-start.1) | collective-permute-done | bytes 1048608 | tf_op jit(solution)/shard_map/ppermute | solution.py:11
  61.8 0.8 fusion.12
  62.6 4.8 %collective-permute-done = bf16[1,1,8,128,512]{4,3,2,1,0:T(8,128)(2,1)S(1)} collective-permute-done((bf16[1,1,8,128,512]{4,3,2,1,0:T(8,128)(2,1)S(1)}, bf16[1,1,8,128,512]{4,3,2,1,0:T(8,128)(2,1)S(1)}, u32[]{:S(2)}, u32[]{:S(2)}) %collective-permute-start) | collective-permute-done | bytes 1048608 | tf_op jit(solution)/shard_map/ppermute | solution.py:11
  67.4 0.8 fusion.6
  68.2 1.6 %collective-permute-start.2 = (f32[27,16,128]{2,1,0:T(8,128)S(1)}, f32[27,16,128]{2,1,0:T(8,128)S(1)}, u32[]{:S(2)}, u32[]{:S(2)}) collective-permute-start(f32[27,16,128]{2,1,0:T(8,128)S(1)} %bitcast.154), channel_id=1, source_target_pairs={{0,1},{1,0},{2,3},{3,2},{4,5},{5,4},{6,7},{7,6},{8,9},{9,8},{10,11... | collective-permute-start | bytes 663560 | tf_op jit(solution)/shard_map/ppermute | solution.py:16
  69.9 0.4 convolution_bitcast_fusion.4
  70.3 0.4 convolution_bitcast_fusion.5
  70.7 0.4 fusion.51
  71.1 0.4 convolution_bitcast_fusion.1
  72.0 2.3 %collective-permute-done.2 = f32[27,16,128]{2,1,0:T(8,128)S(1)} collective-permute-done((f32[27,16,128]{2,1,0:T(8,128)S(1)}, f32[27,16,128]{2,1,0:T(8,128)S(1)}, u32[]{:S(2)}, u32[]{:S(2)}) %collective-permute-start.2) | collective-permute-done | bytes 221216 | tf_op jit(solution)/shard_map/ppermute | solution.py:16
  74.4 0.4 fusion.57
  74.8 0.4 convolution_bitcast_fusion.3
  75.3 5.1 %collective-permute-done.3 = f32[27,16,128]{2,1,0:T(8,128)S(1)} collective-permute-done((f32[27,16,128]{2,1,0:T(8,128)S(1)}, f32[27,16,128]{2,1,0:T(8,128)S(1)}, u32[]{:S(2)}, u32[]{:S(2)}) %collective-permute-start.3) | collective-permute-done | bytes 221216 | tf_op jit(solution)/shard_map/ppermute | solution.py:16
  80.4 0.5 collective-permute-start.4
  81.1 0.4 convolution_bitcast_fusion
  81.5 6.4 %collective-permute-done.4 = f32[27,16,128]{2,1,0:T(8,128)S(1)} collective-permute-done((f32[27,16,128]{2,1,0:T(8,128)S(1)}, f32[27,16,128]{2,1,0:T(8,128)S(1)}, u32[]{:S(2)}, u32[]{:S(2)}) %collective-permute-start.4) | collective-permute-done | bytes 221216 | tf_op jit(solution)/shard_map/ppermute | solution.py:16
  88.2 16.9 %collective-permute-done.5 = f32[27,16,128]{2,1,0:T(8,128)S(1)} collective-permute-done((f32[27,16,128]{2,1,0:T(8,128)S(1)}, f32[27,16,128]{2,1,0:T(8,128)S(1)}, u32[]{:S(2)}, u32[]{:S(2)}) %collective-permute-start.5) | collective-permute-done | bytes 221216 | tf_op jit(solution)/shard_map/ppermute | solution.py:16
  105.2 3.4 %fusion.41 = bf16[1,2,8,16,512]{4,3,2,1,0:T(8,128)(2,1)} fusion(f32[1,2,8,16,512]{4,3,2,1,0:T(8,128)S(1)} %get-tuple-element.26, f32[1,2,8,16,512]{4,3,2,1,0:T(8,128)S(1)} %get-tuple-element.27, f32[1,2,8,16,512]{4,3,2,1,0:T(8,128)S(1)} %get-tuple-element.25, f32[1,2,8,16,512]{4,3,2,1,0:T(8,128)S(1)} %get-tuple-element.41, ...), kind=kLoop, calls=%fused_computation.70 | loop fusion | flops 3538944 | bytes 14417920 | tf_op jit(solution)/shard_map/convert_element_type | solution.py:65
  108.6 6.5 %collective-permute-done.6 = f32[27,16,128]{2,1,0:T(8,128)S(1)} collective-permute-done((f32[27,16,128]{2,1,0:T(8,128)S(1)}, f32[27,16,128]{2,1,0:T(8,128)S(1)}, u32[]{:S(2)}, u32[]{:S(2)}) %collective-permute-start.6) | collective-permute-done | bytes 221216 | tf_op jit(solution)/shard_map/ppermute | solution.py:16
  115.0 0.7 add_multiply_fusion
  (30 shorter events, 2.6 us)
Async XLA Ops:
  3.2 4.6 %copy-start = (bf16[1,2,8,16,512]{4,3,2,1,0:T(8,128)(2,1)S(1)}, bf16[1,2,8,16,512]{4,3,2,1,0:T(8,128)(2,1)}, u32[]{:S(2)}) copy-start(bf16[1,2,8,16,512]{4,3,2,1,0:T(8,128)(2,1)} %param.3) | copy-start | bytes 786436
  3.2 31.8 %all-to-all-start = ((bf16[8,1,2,8,16,512]{5,4,3,2,1,0:T(8,128)(2,1)}), bf16[8,1,2,8,16,512]{5,4,3,2,1,0:T(8,128)(2,1)S(1)}, u32[]{:S(2)}, u32[]{:S(2)}) async-start(bf16[8,1,2,8,16,512]{5,4,3,2,1,0:T(8,128)(2,1)} %stack.2), calls=%async_computation | async-start | bytes 4194304 | tf_op jit(solution)/shard_map/all_to_all | solution.py:36
  7.9 2.2 %copy-start.3 = (bf16[27,16,128]{2,1,0:T(8,128)(2,1)S(1)}, bf16[27,16,128]{2,1,0:T(8,128)(2,1)}, u32[]{:S(2)}) copy-start(bf16[27,16,128]{2,1,0:T(8,128)(2,1)} %param.5) | copy-start | bytes 331780
  8.7 1.4 %copy-start.1 = (bf16[1,2,8,144,512]{4,3,2,1,0:T(8,128)(2,1)}, bf16[1,2,8,144,512]{4,3,2,1,0:T(8,128)(2,1)S(1)}, u32[]{:S(2)}) copy-start(bf16[1,2,8,144,512]{4,3,2,1,0:T(8,128)(2,1)S(1)} %fusion.49) | copy-start | bytes 7077892
  35.3 26.5 %collective-permute-start.1 = (bf16[1,1,8,128,512]{4,3,2,1,0:T(8,128)(2,1)S(1)}, bf16[1,1,8,128,512]{4,3,2,1,0:T(8,128)(2,1)S(1)}, u32[]{:S(2)}, u32[]{:S(2)}) collective-permute-start(bf16[1,1,8,128,512]{4,3,2,1,0:T(8,128)(2,1)S(1)} %get-tuple-element.2), channel_id=1, source_target_pairs={{0,16},{16,32},{32,48},{48,64},{64,80},{80,96},{96,112},{112,128},... | collective-permute-start | bytes 3145736 | tf_op jit(solution)/shard_map/ppermute | solution.py:11
  37.3 30.1 %collective-permute-start = (bf16[1,1,8,128,512]{4,3,2,1,0:T(8,128)(2,1)S(1)}, bf16[1,1,8,128,512]{4,3,2,1,0:T(8,128)(2,1)S(1)}, u32[]{:S(2)}, u32[]{:S(2)}) collective-permute-start(bf16[1,1,8,128,512]{4,3,2,1,0:T(8,128)(2,1)S(1)} %get-tuple-element.3), channel_id=1, source_target_pairs={{16,0},{32,16},{48,32},{64,48},{80,64},{96,80},{112,96},{128,112},... | collective-permute-start | bytes 3145736 | tf_op jit(solution)/shard_map/ppermute | solution.py:11
  42.6 1.7 %copy-start.2 = (bf16[1,2,8,144,512]{4,3,2,1,0:T(8,128)(2,1)S(1)}, bf16[1,2,8,144,512]{4,3,2,1,0:T(8,128)(2,1)}, u32[]{:S(2)}) copy-start(bf16[1,2,8,144,512]{4,3,2,1,0:T(8,128)(2,1)} %copy-done.1) | copy-start | bytes 7077892
  68.2 6.1 %collective-permute-start.2 = (f32[27,16,128]{2,1,0:T(8,128)S(1)}, f32[27,16,128]{2,1,0:T(8,128)S(1)}, u32[]{:S(2)}, u32[]{:S(2)}) collective-permute-start(f32[27,16,128]{2,1,0:T(8,128)S(1)} %bitcast.154), channel_id=1, source_target_pairs={{0,1},{1,0},{2,3},{3,2},{4,5},{5,4},{6,7},{7,6},{8,9},{9,8},{10,11... | collective-permute-start | bytes 663560 | tf_op jit(solution)/shard_map/ppermute | solution.py:16
  74.3 6.0 %collective-permute-start.3 = (f32[27,16,128]{2,1,0:T(8,128)S(1)}, f32[27,16,128]{2,1,0:T(8,128)S(1)}, u32[]{:S(2)}, u32[]{:S(2)}) collective-permute-start(f32[27,16,128]{2,1,0:T(8,128)S(1)} %add.183), channel_id=1, source_target_pairs={{0,16},{16,0},{32,48},{48,32},{64,80},{80,64},{96,112},{112,96},{1... | collective-permute-start | bytes 663560 | tf_op jit(solution)/shard_map/ppermute | solution.py:16
  80.4 7.5 %collective-permute-start.4 = (f32[27,16,128]{2,1,0:T(8,128)S(1)}, f32[27,16,128]{2,1,0:T(8,128)S(1)}, u32[]{:S(2)}, u32[]{:S(2)}) collective-permute-start(f32[27,16,128]{2,1,0:T(8,128)S(1)} %add.184), channel_id=1, source_target_pairs={{0,128},{16,144},{32,160},{48,176},{64,192},{80,208},{96,224},{112... | collective-permute-start | bytes 663560 | tf_op jit(solution)/shard_map/ppermute | solution.py:16
  87.9 17.2 %collective-permute-start.5 = (f32[27,16,128]{2,1,0:T(8,128)S(1)}, f32[27,16,128]{2,1,0:T(8,128)S(1)}, u32[]{:S(2)}, u32[]{:S(2)}) collective-permute-start(f32[27,16,128]{2,1,0:T(8,128)S(1)} %add.185), channel_id=1, source_target_pairs={{0,32},{16,48},{32,0},{48,16},{64,96},{80,112},{96,64},{112,80},{1... | collective-permute-start | bytes 663560 | tf_op jit(solution)/shard_map/ppermute | solution.py:16
  105.1 9.9 %collective-permute-start.6 = (f32[27,16,128]{2,1,0:T(8,128)S(1)}, f32[27,16,128]{2,1,0:T(8,128)S(1)}, u32[]{:S(2)}, u32[]{:S(2)}) collective-permute-start(f32[27,16,128]{2,1,0:T(8,128)S(1)} %add.186), channel_id=1, source_target_pairs={{0,64},{16,80},{32,96},{48,112},{64,0},{80,16},{96,32},{112,48},{1... | collective-permute-start | bytes 663560 | tf_op jit(solution)/shard_map/ppermute | solution.py:16
